TPU v7x, 512 devices: a whole 4x8x8 slice. The times are simulated.
512 devices in a mesh: dp: 16 (over z_hi, y), tensor: 32 (over x, z_lo, core).
Axes of the slice: x: 4, y: 8, z: 8 (z_hi: 2, z_lo: 4; z = z_hi * 4 + z_lo), core: 2. Of those that a mesh axis runs over, the one named last changes fastest.
Arguments:
- suffix_states: bfloat16 [32, 128, 2048], P(None, 'dp', 'tensor'), may hold values from -16 to 16
- suffix_lengths: int32 [32], replicated, may hold values from 1 to 128, 2560 in all
- request_group: int32 [32, 1], replicated, may hold values from 0 to 15
- group_owner: int32 [16], replicated, may hold values from 0 to 15, each once
- request_order: int32 [32], replicated, may hold values from 0 to 31, each once
- prefix_cache: bfloat16 [16, 256, 1024], P('dp', 'tensor'), may hold values from -700 to 700
- norm_attn: bfloat16 [2048], replicated, may hold values from 0.099609375 to 1.8984375
- w_query: bfloat16 [2048, 2048], P(None, 'tensor'), may hold values from -0.125 to 0.125
- w_key: bfloat16 [2048, 512], P(None, 'tensor'), may hold values from -0.125 to 0.125
- w_value: bfloat16 [2048, 512], P(None, 'tensor'), may hold values from -0.125 to 0.125
- w_out: bfloat16 [2048, 2048], P('tensor'), may hold values from -0.25 to 0.25
- norm_mlp: bfloat16 [2048], replicated, may hold values from 0.099609375 to 1.8984375
- w_gate: bfloat16 [2048, 8192], P(None, 'tensor'), may hold values from -0.125 to 0.125
- w_up: bfloat16 [2048, 8192], P(None, 'tensor'), may hold values from -0.125 to 0.125
- w_down: bfloat16 [8192, 2048], P('tensor'), may hold values from -0.125 to 0.125
Outputs:
- hidden_out: bfloat16 [32, 128, 2048], P(None, 'dp', 'tensor')
- suffix_keys: bfloat16 [32, 128, 512], P('dp', None, 'tensor')
- suffix_values: bfloat16 [32, 128, 512], P('dp', None, 'tensor')
Inputs may be any that keep to these rules, and one draw needn't show every extreme that they name: `suffix_lengths`: the lengths sum to 2560 and some request has exactly 128. `request_group`: every group has at least one request. `group_owner`: A permutation of the 16 groups onto the slots of prefix_cache. `request_order`: A permutation of the requests; slot s belongs to index s // 2 of dp.
All inputs are finite; a program needn't handle non-finite values.
Results may differ from a plain program's by a relative error of at most 0.03.
Values may be sent and summed in bfloat16 or wider, within the bound.
No kernel may reach another device: no remote copies, remote signals or barrier semaphores. Data moves between devices by JAX's collectives and lax.ppermute only.
A program may use at most 64 MiB of HBM per device.

v0:
```python
import jax
import jax.numpy as jnp
import numpy as np
from jax import lax
from jax.sharding import PartitionSpec as P

H = 32
KVH = 8
HD = 64
L_MAX = 128
P_SIZE = 256
THETA = 10000000.0
EPSILON = 1e-05


def rms_scale(states, gain):
    wide = states.astype(jnp.float32)
    mean_square = jnp.mean(wide * wide, axis=-1, keepdims=True)
    return (wide * lax.rsqrt(mean_square + EPSILON) * gain.astype(jnp.float32)).astype(jnp.bfloat16)


def rotate(vectors, positions):
    half = HD // 2
    freqs = THETA ** (-(jnp.arange(half, dtype=jnp.float32) * 2.0 / HD))
    angles = positions[:, None] * freqs[None, :]
    cosine = jnp.cos(angles)[:, None, :]
    sine = jnp.sin(angles)[:, None, :]
    first = vectors[..., :half]
    second = vectors[..., half:]
    return jnp.concatenate(
        [first * cosine - second * sine, second * cosine + first * sine], axis=-1
    )


def absorb_block(state_now, scores, allowed, value_rows):
    running_max, running_sum, numerator = state_now
    block_max = jnp.max(jnp.where(allowed, scores, -1e30), axis=2)
    new_max = jnp.maximum(running_max, block_max)
    rescale = jnp.exp(running_max - new_max)
    weights = jnp.where(allowed, jnp.exp(scores - new_max[:, :, None]), 0.0)
    running_sum = running_sum * rescale + jnp.sum(weights, axis=2)
    numerator = numerator * rescale[:, :, None] + jnp.einsum(
        "htk,khd->htd", weights.astype(jnp.bfloat16), value_rows, preferred_element_type=jnp.float32
    )
    return (new_max, running_sum, numerator)


def shards(
    suffix_states,
    suffix_lengths,
    request_group,
    group_owner,
    request_order,
    prefix_cache,
    norm_attn,
    w_query,
    w_key,
    w_value,
    w_out,
    norm_mlp,
    w_gate,
    w_up,
    w_down,
):
    dp_count = lax.axis_size("dp")
    tp_count = lax.axis_size("tensor")
    dp_index = lax.axis_index("dp")
    tp_index = lax.axis_index("tensor")
    total_reqs = suffix_lengths.shape[0]
    local_reqs = total_reqs // dp_count
    row_count = local_reqs * L_MAX
    heads_here = w_query.shape[1] // HD
    group_size = H // KVH
    kv_here = max(1, heads_here // group_size)
    slab_width = kv_here * 2 * HD
    score_scale = HD ** (-0.5)
    head_map = np.arange(heads_here) // group_size
    dest_table = (
        np.arange(tp_count)[:, None] * heads_here // group_size + np.arange(kv_here)[None, :]
    ).reshape(-1)
    routed = jnp.take(suffix_states, request_order, axis=0)
    routed_here = lax.all_to_all(routed, "dp", split_axis=0, concat_axis=1, tiled=True)
    width_here = routed_here.shape[2]
    state_shard = routed_here.reshape(row_count, width_here)
    slot_ids = dp_index * local_reqs + jnp.arange(local_reqs, dtype=jnp.int32)
    req_ids = jnp.take(request_order, slot_ids)
    lengths_here = jnp.take(suffix_lengths, req_ids)
    owner_here = jnp.take(group_owner, jnp.take(request_group[:, 0], req_ids))
    position = jnp.arange(L_MAX, dtype=jnp.int32)
    valid = (position[None, :] < lengths_here[:, None]).reshape(row_count)
    positions = (P_SIZE + jnp.tile(position, local_reqs)).astype(jnp.float32)
    full_rows = lax.all_gather(state_shard, "tensor", axis=1, tiled=True)
    normed = rms_scale(full_rows, norm_attn)
    query = rotate(
        jnp.dot(normed, w_query, preferred_element_type=jnp.float32).reshape(
            row_count, heads_here, HD
        ),
        positions,
    ).astype(jnp.bfloat16)
    key_part = jnp.dot(normed, w_key, preferred_element_type=jnp.float32).astype(jnp.bfloat16)
    value_part = jnp.dot(normed, w_value, preferred_element_type=jnp.float32).astype(jnp.bfloat16)
    key_full, value_full = (
        lax.all_gather(key_part, "tensor", axis=1, tiled=True),
        lax.all_gather(value_part, "tensor", axis=1, tiled=True),
    )
    key_heads = key_full.reshape(row_count, HD, KVH).transpose(0, 2, 1)
    value_heads = value_full.reshape(row_count, HD, KVH).transpose(0, 2, 1)
    key_rot = rotate(key_heads.astype(jnp.float32), positions).astype(jnp.bfloat16)
    cache_width = key_part.shape[1]
    keys_flat = jnp.where(valid[:, None], key_rot.reshape(row_count, KVH * HD), 0.0)
    values_flat = jnp.where(valid[:, None], value_heads.reshape(row_count, KVH * HD), 0.0)
    keys_out = lax.dynamic_slice_in_dim(keys_flat, tp_index * cache_width, cache_width, 1).reshape(
        local_reqs, L_MAX, cache_width
    )
    values_out = lax.dynamic_slice_in_dim(
        values_flat, tp_index * cache_width, cache_width, 1
    ).reshape(local_reqs, L_MAX, cache_width)
    kv_first = tp_index * heads_here // group_size
    own_keys = lax.dynamic_slice_in_dim(key_rot, kv_first, kv_here, 1)[:, head_map].reshape(
        local_reqs, L_MAX, heads_here, HD
    )
    own_values = lax.dynamic_slice_in_dim(value_heads, kv_first, kv_here, 1)[:, head_map].reshape(
        local_reqs, L_MAX, heads_here, HD
    )
    query_req = query.reshape(local_reqs, L_MAX, heads_here, HD)

    def absorb_prefix(state_one, query_one, slot_block):
        block = slot_block.reshape(slot_block.shape[0], kv_here, 2, HD)
        key_rows = block[:, head_map, 0]
        value_rows = block[:, head_map, 1]
        scores = (
            jnp.einsum("thd,phd->htp", query_one, key_rows, preferred_element_type=jnp.float32)
            * score_scale
        )
        return absorb_block(state_one, scores, jnp.ones((1, 1, 1), bool), value_rows)

    initial = tuple(
        (
            (
                jnp.full((heads_here, L_MAX), -1e30, jnp.float32),
                jnp.zeros((heads_here, L_MAX), jnp.float32),
                jnp.zeros((heads_here, L_MAX, HD), jnp.float32),
            )
            for request in range(local_reqs)
        )
    )
    all_rows = lax.all_gather(prefix_cache, "dp", axis=0, tiled=True)
    rows_each = all_rows.shape[1]
    chosen = jnp.take(all_rows.reshape(dp_count, rows_each, KVH, 2 * HD), dest_table, axis=2)
    picked = lax.all_to_all(chosen, "tensor", split_axis=2, concat_axis=1, tiled=True).reshape(
        dp_count, P_SIZE, slab_width
    )
    states = tuple(
        (
            absorb_prefix(
                initial[request],
                query_req[request],
                lax.dynamic_index_in_dim(picked, owner_here[request], 0, keepdims=False),
            )
            for request in range(local_reqs)
        )
    )
    pieces = []
    for request in range(local_reqs):
        self_scores = (
            jnp.einsum(
                "thd,shd->hts",
                query_req[request],
                own_keys[request],
                preferred_element_type=jnp.float32,
            )
            * score_scale
        )
        self_allowed = (position[None, :] <= position[:, None]) & (
            position[None, :] < lengths_here[request]
        )
        running_max, running_sum, numerator = absorb_block(
            states[request], self_scores, self_allowed[None], own_values[request]
        )
        attention_one = (numerator / running_sum[:, :, None]).astype(jnp.bfloat16)
        pieces.append(attention_one.transpose(1, 0, 2).reshape(L_MAX, heads_here * HD))
    attention = jnp.concatenate(pieces, axis=0)
    attn_terms = jnp.dot(attention, w_out, preferred_element_type=jnp.float32)
    attn_share = lax.psum_scatter(
        attn_terms.astype(jnp.bfloat16), "tensor", scatter_dimension=1, tiled=True
    ).astype(jnp.float32)
    middle = (state_shard.astype(jnp.float32) + attn_share).astype(jnp.bfloat16)
    middle_rows = lax.all_gather(middle, "tensor", axis=1, tiled=True)
    normed_two = rms_scale(middle_rows, norm_mlp)
    gate = jnp.dot(normed_two, w_gate, preferred_element_type=jnp.float32)
    upper = jnp.dot(normed_two, w_up, preferred_element_type=jnp.float32)
    hidden = (jax.nn.silu(gate) * upper).astype(jnp.bfloat16)
    down_terms = jnp.dot(hidden, w_down, preferred_element_type=jnp.float32)
    down_share = lax.psum_scatter(
        down_terms.astype(jnp.bfloat16), "tensor", scatter_dimension=1, tiled=True
    ).astype(jnp.float32)
    result = middle.astype(jnp.float32) + down_share
    result = (
        jnp.where(valid[:, None], result, 0.0)
        .astype(jnp.bfloat16)
        .reshape(local_reqs, L_MAX, width_here)
    )
    returned = lax.all_to_all(result, "dp", split_axis=1, concat_axis=0, tiled=True)
    hidden_out = jnp.zeros_like(returned).at[request_order].set(returned)
    return (hidden_out, keys_out, values_out)


def solution(mesh):
    in_specs = (
        P(None, "dp", "tensor"),
        P(),
        P(),
        P(),
        P(),
        P("dp", "tensor", None),
        P(),
        P(None, "tensor"),
        P(None, "tensor"),
        P(None, "tensor"),
        P("tensor", None),
        P(),
        P(None, "tensor"),
        P(None, "tensor"),
        P("tensor", None),
    )
    out_specs = (P(None, "dp", "tensor"), P("dp", None, "tensor"), P("dp", None, "tensor"))
    return jax.shard_map(shards, mesh=mesh, in_specs=in_specs, out_specs=out_specs, check_vma=False)
```

profile of v0, /device:TPU:8, one launch (start us, length us, event | category | flops | bytes accessed | tf_op | source)
XLA Modules:
  0.0 635.4 jit_solution(12212164289237570744)
XLA Ops:
  7.2 0.7 compare_select_fusion.3
  7.9 0.7 compare_and_fusion.1
  8.6 1.4 gather_fusion
  10.1 0.7 reshape.707
  10.9 16.0 %all-to-all-start = ((bf16[16,2,512]{2,1,0:T(2,128)(2,1)}), bf16[16,2,512]{2,1,0:T(2,128)(2,1)S(1)}, u32[]{:S(2)}, u32[]{:S(2)}) async-start(bf16[16,2,512]{2,1,0:T(2,128)(2,1)} %reshape.707), calls=%async_computation | async-start | bytes 65536 | tf_op jit(solution)/shard_map/all_to_all | solution.py:82
  26.9 49.1 %all_gather.16 = bf16[16,8,1024]{2,1,0:T(8,128)(2,1)S(1)} all-gather(bf16[1,8,1024]{2,1,0:T(8,128)(2,1)} %param.30), channel_id=1, replica_groups=mesh['dp'=16,'tensor'=32] {'dp'}, dimensions={0}, use_global_device_ids=true | all-gather | bytes 278528 | tf_op jit(solution)/shard_map/all_gather | solution.py:147
  76.0 0.7 pad_clamp_fusion.1
  76.7 1.9 gather_fusion.1
  78.6 6.7 %all-to-all-start.1 = ((bf16[16,8,32,128]{3,1,0,2:T(8,128)(2,1)}), bf16[16,8,32,128]{3,1,0,2:T(8,128)(2,1)S(1)}, u32[]{:S(2)}, u32[]{:S(2)}) async-start(bf16[16,8,32,128]{3,1,0,2:T(8,128)(2,1)} %bitcast.9), calls=%async_computation.1 | async-start | bytes 2097152 | tf_op jit(solution)/shard_map/all_to_all | solution.py:150
  85.4 0.6 gather_fusion.3
  86.1 0.7 copy.51
  87.0 0.6 gather_fusion.5
  87.6 0.6 gather_fusion.4
  88.3 0.6 gather_fusion.2
  88.9 0.6 fusion.81
  93.5 0.6 fusion.80
  94.1 0.6 iota_compare_fusion.2
  94.7 0.7 iota_compare_fusion.1
  95.6 17.5 %all-to-all-done.1 = bf16[16,8,32,128]{3,1,0,2:T(8,128)(2,1)S(1)} async-done(((bf16[16,8,32,128]{3,1,0,2:T(8,128)(2,1)}), bf16[16,8,32,128]{3,1,0,2:T(8,128)(2,1)S(1)}, u32[]{:S(2)}, u32[]{:S(2)}) %all-to-all-start.1) | async-done | bytes 1048608 | tf_op jit(solution)/shard_map/all_to_all | solution.py:150
  113.1 0.3 copy_bitcast_fusion
  113.6 37.2 %all-gather.3.cloned.1.call-done = bf16[256,2048]{0,1:T(8,128)(2,1)} async-done(((bf16[256,64]{0,1:T(8,128)(2,1)}), bf16[256,2048]{0,1:T(8,128)(2,1)}) %all-gather.3.cloned.1.call-update) | async-done | bytes 1048592 | tf_op jit(solution)/shard_map/all_gather | solution.py:92
  150.8 1.6 fusion
  152.5 0.5 convolution_bitcast_fusion
  153.3 0.5 convolution_convert_fusion.2
  153.8 41.5 %all_gather.18 = bf16[256,512]{0,1:T(8,128)(2,1)S(1)} all-gather(bf16[256,16]{0,1:T(8,128)(2,1)S(1)} %convolution_convert_fusion.2), channel_id=1, replica_groups=mesh['dp'=16,'tensor'=32] {'tensor'}, dimensions={1}, use_global_device_ids=true | all-gather | bytes 270336 | tf_op jit(solution)/shard_map/all_gather | solution.py:104
  195.4 0.5 convolution_convert_fusion.3
  195.8 38.9 %all_gather.17 = bf16[256,512]{0,1:T(8,128)(2,1)S(1)} all-gather(bf16[256,16]{0,1:T(8,128)(2,1)S(1)} %convolution_convert_fusion.3), channel_id=1, replica_groups=mesh['dp'=16,'tensor'=32] {'tensor'}, dimensions={1}, use_global_device_ids=true | all-gather | bytes 270336 | tf_op jit(solution)/shard_map/all_gather | solution.py:103
  235.0 0.3 fusion.82
  235.2 0.3 fusion.83
  235.7 0.2 select_reduce_fusion.1
  235.9 0.2 select_reduce_fusion
  237.0 0.2 fusion.10
  237.2 0.2 fusion.12
  237.7 1.5 convolution_convert_fusion.1
  239.2 147.1 %reduce-scatter.3.cloned.1.call-done = bf16[256,64]{0,1:T(8,128)(2,1)} async-done(((bf16[256,2048]{0,1:T(8,128)(2,1)}), bf16[256,64]{0,1:T(8,128)(2,1)}) %reduce-scatter.3.cloned.1.call-update) | async-done | bytes 32784 | tf_op jit(solution)/shard_map/reduce_scatter | solution.py:184
  386.3 1.4 add_convert_fusion
  387.8 59.3 %all-gather.5.cloned.1.call-done = bf16[256,2048]{0,1:T(8,128)(2,1)} async-done(((bf16[256,64]{0,1:T(8,128)(2,1)}), bf16[256,2048]{0,1:T(8,128)(2,1)}) %all-gather.5.cloned.1.call-update) | async-done | bytes 1048592 | tf_op jit(solution)/shard_map/all_gather | solution.py:188
  447.1 1.6 fusion.3
  448.8 2.1 fusion.15
  450.9 4.1 convolution_convert_fusion
  455.1 148.5 %reduce-scatter.5.cloned.1.call-done = bf16[256,64]{0,1:T(8,128)(2,1)} async-done(((bf16[256,2048]{0,1:T(8,128)(2,1)}), bf16[256,64]{0,1:T(8,128)(2,1)}) %reduce-scatter.5.cloned.1.call-update) | async-done | bytes 32784 | tf_op jit(solution)/shard_map/reduce_scatter | solution.py:194
  603.6 0.8 select_convert_fusion
  604.5 0.7 reshape.709
  605.2 10.2 %all-to-all-start.2 = ((bf16[16,2,512]{2,1,0:T(2,128)(2,1)}), bf16[16,2,512]{2,1,0:T(2,128)(2,1)S(1)}, u32[]{:S(2)}, u32[]{:S(2)}) async-start(bf16[16,2,512]{2,1,0:T(2,128)(2,1)} %reshape.709), calls=%async_computation.4 | async-start | bytes 65536 | tf_op jit(solution)/shard_map/all_to_all | solution.py:203
  615.4 0.6 copy_bitcast_fusion.3
  616.0 10.5 %all-to-all-done.2 = bf16[16,2,512]{2,1,0:T(2,128)(2,1)S(1)} async-done(((bf16[16,2,512]{2,1,0:T(2,128)(2,1)}), bf16[16,2,512]{2,1,0:T(2,128)(2,1)S(1)}, u32[]{:S(2)}, u32[]{:S(2)}) %all-to-all-start.2) | async-done | bytes 32800 | tf_op jit(solution)/shard_map/all_to_all | solution.py:203
  626.8 1.5 scatter_fusion
  628.3 0.6 copy-done.9
  (85 shorter events, 3.1 us)
Async XLA Ops:
  7.2 443.7 %copy-start = (bf16[256,2048]{1,0:T(8,128)(2,1)S(1)}, bf16[256,2048]{1,0:T(8,128)(2,1)}, u32[]{:S(2)}) copy-start(bf16[256,2048]{1,0:T(8,128)(2,1)} %param.39) | copy-start | bytes 3145732
  10.9 67.7 %all-to-all-start = ((bf16[16,2,512]{2,1,0:T(2,128)(2,1)}), bf16[16,2,512]{2,1,0:T(2,128)(2,1)S(1)}, u32[]{:S(2)}, u32[]{:S(2)}) async-start(bf16[16,2,512]{2,1,0:T(2,128)(2,1)} %reshape.707), calls=%async_computation | async-start | bytes 65536 | tf_op jit(solution)/shard_map/all_to_all | solution.py:82
  78.6 6.8 %copy-start.1 = (s32[32]{0:T(128)S(1)}, s32[32]{0:T(128)}, u32[]{:S(2)}) copy-start(s32[32]{0:T(128)} %param.29) | copy-start | bytes 388
  78.6 8.4 %copy-start.2 = (s32[32,1]{0,1:T(1,128)S(1)}, s32[32,1]{0,1:T(1,128)}, u32[]{:S(2)}) copy-start(s32[32,1]{0,1:T(1,128)} %param.27) | copy-start | bytes 388
  78.6 34.5 %all-to-all-start.1 = ((bf16[16,8,32,128]{3,1,0,2:T(8,128)(2,1)}), bf16[16,8,32,128]{3,1,0,2:T(8,128)(2,1)S(1)}, u32[]{:S(2)}, u32[]{:S(2)}) async-start(bf16[16,8,32,128]{3,1,0,2:T(8,128)(2,1)} %bitcast.9), calls=%async_computation.1 | async-start | bytes 2097152 | tf_op jit(solution)/shard_map/all_to_all | solution.py:150
  85.3 2.4 copy-start.3
  85.3 3.0 copy-start.4
  85.3 65.6 %all-gather.3.cloned.1.call-start = ((), (), s32[]{:S(2)}) async-start(), calls=%async_computation.5 | async-start | bytes 1081344 | tf_op jit(solution)/shard_map/all_gather | solution.py:92
  86.0 6.1 copy-start.11
  86.9 299.5 %reduce-scatter.3.cloned.1.call-start = ((), (), s32[]{:S(2)}) async-start(), calls=%async_computation.6 | async-start | bytes 1081344 | tf_op jit(solution)/shard_map/reduce_scatter | solution.py:184
  113.4 39.1 %copy-start.13 = (bf16[2048,64]{0,1:T(8,128)(2,1)S(1)}, bf16[2048,64]{0,1:T(8,128)(2,1)}, u32[]{:S(2)}) copy-start(bf16[2048,64]{0,1:T(8,128)(2,1)} %param.32) | copy-start | bytes 786436
  150.8 1.6 copy-start.5
  152.5 0.8 copy-start.14
  153.3 42.0 %copy-start.15 = (bf16[2048,16]{0,1:T(8,128)(2,1)S(1)}, bf16[2048,16]{0,1:T(8,128)(2,1)}, u32[]{:S(2)}) copy-start(bf16[2048,16]{0,1:T(8,128)(2,1)} %param.33) | copy-start | bytes 196612
  235.6 2.1 copy-start.10
  237.7 148.7 %copy-start.7 = (bf16[256,64]{0,1:T(8,128)(2,1)S(1)}, bf16[256,64]{0,1:T(8,128)(2,1)}, u32[]{:S(2)}) copy-start(bf16[256,64]{0,1:T(8,128)(2,1)} %copy.51) | copy-start | bytes 98308
  237.7 150.1 %copy-start.12 = (bf16[2048]{0:T(1024)(128)(2,1)S(1)}, bf16[2048]{0:T(1024)(128)(2,1)}, u32[]{:S(2)}) copy-start(bf16[2048]{0:T(1024)(128)(2,1)} %param.36) | copy-start | bytes 12292
  239.2 207.9 %all-gather.5.cloned.1.call-start = ((), (), s32[]{:S(2)}) async-start(), calls=%async_computation.7 | async-start | bytes 1081344 | tf_op jit(solution)/shard_map/all_gather | solution.py:188
  387.7 215.8 %reduce-scatter.5.cloned.1.call-start = ((), (), s32[]{:S(2)}) async-start(), calls=%async_computation.8 | async-start | bytes 1081344 | tf_op jit(solution)/shard_map/reduce_scatter | solution.py:194
  447.1 1.6 copy-start.6
  454.9 148.7 %copy-start.8 = (bf16[256,64]{0,1:T(8,128)(2,1)S(1)}, bf16[256,64]{0,1:T(8,128)(2,1)}, u32[]{:S(2)}) copy-start(bf16[256,64]{0,1:T(8,128)(2,1)} %add_convert_fusion) | copy-start | bytes 98308
  605.2 21.4 %all-to-all-start.2 = ((bf16[16,2,512]{2,1,0:T(2,128)(2,1)}), bf16[16,2,512]{2,1,0:T(2,128)(2,1)S(1)}, u32[]{:S(2)}, u32[]{:S(2)}) async-start(bf16[16,2,512]{2,1,0:T(2,128)(2,1)} %reshape.709), calls=%async_computation.4 | async-start | bytes 65536 | tf_op jit(solution)/shard_map/all_to_all | solution.py:203
  628.3 0.6 copy-start.9
Sparse Core Ops, SparseCore 0:
  88.8 61.9 all-gather.2
  239.3 146.9 reduce-scatter.2
  389.1 58.0 all-gather.4
  455.1 148.4 reduce-scatter.4
where the time goes:
time: 636 us; the launch traced here: 635 us
  waiting for transfers between devices  420 us (66%)
  blocking collectives  130 us (20%)
  starting transfers between devices  33.1 us (5%)
  between operations  18.1 us (3%)
  local copies, waits for them, and re-layouts  13.2 us (2%)
  matrix products  11 us (2%)
  other arithmetic  10.2 us (2%)
    reduce_scatter x1, waiting for transfers between devices, shards(): lax.psum_scatter(down_terms.astype(jnp.bfloat16), 'tensor', scatter_dimen...  149 us
    reduce_scatter x1, waiting for transfers between devices, shards(): lax.psum_scatter(attn_terms.astype(jnp.bfloat16), 'tensor', scatter_dimen...  147 us
    all_gather x1, waiting for transfers between devices, shards(): middle_rows = lax.all_gather(middle, 'tensor', axis=1, tiled=True)  59.3 us
    all_gather x1, blocking collectives, shards(): all_rows = lax.all_gather(prefix_cache, 'dp', axis=0, tiled=True)  49.1 us
    all_gather x1, blocking collectives, shards(): lax.all_gather(value_part, 'tensor', axis=1, tiled=True)  41.5 us
    all_gather x1, blocking collectives, shards(): lax.all_gather(key_part, 'tensor', axis=1, tiled=True)  38.9 us
    all_gather x1, waiting for transfers between devices, shards(): full_rows = lax.all_gather(state_shard, 'tensor', axis=1, tiled=True)  37.2 us
    all_to_all x1, waiting for transfers between devices, shards(): lax.all_to_all(chosen, 'tensor', split_axis=2, concat_axis=1, tiled=True)  17.5 us
  transfers between devices with their start and end apart: 7, of which 6 were waited for; matrix products, arithmetic and copies ran while one was open for 2% of the time, Pallas kernels for 0%

commit v1 on v0

--- a/solution.py
+++ b/solution.py
@@ -11,6 +11,15 @@
 P_SIZE = 256
 THETA = 10000000.0
 EPSILON = 1e-05
+corner_apply = lambda local_array: jnp.concatenate(
+    jax.lax.all_to_all(
+        jnp.stack(jnp.split(local_array, jax.lax.axis_size("dp"), axis=0), axis=0),
+        "dp",
+        split_axis=0,
+        concat_axis=0,
+    ),
+    axis=1,
+)
 
 
 def rms_scale(states, gain):
@@ -79,7 +88,7 @@
         np.arange(tp_count)[:, None] * heads_here // group_size + np.arange(kv_here)[None, :]
     ).reshape(-1)
     routed = jnp.take(suffix_states, request_order, axis=0)
-    routed_here = lax.all_to_all(routed, "dp", split_axis=0, concat_axis=1, tiled=True)
+    routed_here = corner_apply(routed)
     width_here = routed_here.shape[2]
     state_shard = routed_here.reshape(row_count, width_here)
     slot_ids = dp_index * local_reqs + jnp.arange(local_reqs, dtype=jnp.int32)

time: 636 us -> 638 us (level)
  transfers between devices with their start and end apart: 7 -> 7, of which waited for: 6 -> 6; matrix products, arithmetic and copies ran while one was open for 2% -> 1% of each run, Pallas kernels for 0% -> 0%
where the time goes in v1:
time: 638 us; the launch traced here: 637 us
  waiting for transfers between devices  422 us (66%)
  blocking collectives  129 us (20%)
  starting transfers between devices  33 us (5%)
  between operations  18.2 us (3%)
  local copies, waits for them, and re-layouts  14.4 us (2%)
  matrix products  11 us (2%)
  other arithmetic  9.54 us (1%)
    reduce_scatter x1, waiting for transfers between devices, shards(): lax.psum_scatter(down_terms.astype(jnp.bfloat16), 'tensor', scatter_dimen...  149 us
    reduce_scatter x1, waiting for transfers between devices, shards(): lax.psum_scatter(attn_terms.astype(jnp.bfloat16), 'tensor', scatter_dimen...  147 us
    all_gather x1, waiting for transfers between devices, shards(): middle_rows = lax.all_gather(middle, 'tensor', axis=1, tiled=True)  59.4 us
    all_gather x1, blocking collectives, shards(): all_rows = lax.all_gather(prefix_cache, 'dp', axis=0, tiled=True)  49 us
    all_gather x1, blocking collectives, shards(): lax.all_gather(value_part, 'tensor', axis=1, tiled=True)  41.6 us
    all_gather x1, blocking collectives, shards(): lax.all_gather(key_part, 'tensor', axis=1, tiled=True)  38.9 us
    all_gather x1, waiting for transfers between devices, shards(): full_rows = lax.all_gather(state_shard, 'tensor', axis=1, tiled=True)  37.3 us
    all_to_all x1, waiting for transfers between devices, shards(): lax.all_to_all(chosen, 'tensor', split_axis=2, concat_axis=1, tiled=True)  19.6 us
  transfers between devices with their start and end apart: 7, of which 6 were waited for; matrix products, arithmetic and copies ran while one was open for 1% of the time, Pallas kernels for 0%

profile of v1, /device:TPU:8, one launch (start us, length us, event | category | flops | bytes accessed | tf_op | source)
XLA Modules:
  0.0 637.5 jit_solution(942688094595153524)
XLA Ops:
  7.2 0.7 compare_select_fusion.3
  8.0 0.7 compare_and_fusion.1
  8.6 1.3 gather_fusion.3
  10.0 1.3 gather_fusion.5
  11.3 0.6 gather_fusion.4
  11.9 0.6 gather_fusion
  12.8 0.7 reshape.706
  13.6 16.0 %all-to-all-start = ((bf16[16,2,512]{2,1,0:T(2,128)(2,1)}), bf16[16,2,512]{2,1,0:T(2,128)(2,1)S(1)}, u32[]{:S(2)}, u32[]{:S(2)}) async-start(bf16[16,2,512]{2,1,0:T(2,128)(2,1)} %reshape.706), calls=%async_computation | async-start | bytes 65536 | tf_op jit(solution)/shard_map/all_to_all | solution.py:15
  29.6 49.0 %all_gather.16 = bf16[16,8,1024]{2,1,0:T(8,128)(2,1)S(1)} all-gather(bf16[1,8,1024]{2,1,0:T(8,128)(2,1)S(1)} %copy-done.10), channel_id=1, replica_groups=mesh['dp'=16,'tensor'=32] {'dp'}, dimensions={0}, use_global_device_ids=true | all-gather | bytes 278528 | tf_op jit(solution)/shard_map/all_gather | solution.py:156
  78.5 1.9 gather_fusion.1
  80.4 6.7 %all-to-all-start.1 = ((bf16[16,8,32,128]{3,1,0,2:T(8,128)(2,1)}), bf16[16,8,32,128]{3,1,0,2:T(8,128)(2,1)S(1)}, u32[]{:S(2)}, u32[]{:S(2)}) async-start(bf16[16,8,32,128]{3,1,0,2:T(8,128)(2,1)} %bitcast.23), calls=%async_computation.1 | async-start | bytes 2097152 | tf_op jit(solution)/shard_map/all_to_all | solution.py:159
  87.3 0.7 copy.51
  88.1 0.6 gather_fusion.2
  88.7 0.6 fusion.81
  93.3 0.6 fusion.80
  93.9 0.6 iota_compare_fusion.2
  94.5 0.7 iota_compare_fusion.1
  95.4 19.6 %all-to-all-done.1 = bf16[16,8,32,128]{3,1,0,2:T(8,128)(2,1)S(1)} async-done(((bf16[16,8,32,128]{3,1,0,2:T(8,128)(2,1)}), bf16[16,8,32,128]{3,1,0,2:T(8,128)(2,1)S(1)}, u32[]{:S(2)}, u32[]{:S(2)}) %all-to-all-start.1) | async-done | bytes 1048608 | tf_op jit(solution)/shard_map/all_to_all | solution.py:159
  114.9 0.3 copy_bitcast_fusion
  115.5 37.3 %all-gather.3.cloned.1.call-done = bf16[256,2048]{0,1:T(8,128)(2,1)} async-done(((bf16[256,64]{0,1:T(8,128)(2,1)}), bf16[256,2048]{0,1:T(8,128)(2,1)}) %all-gather.3.cloned.1.call-update) | async-done | bytes 1048592 | tf_op jit(solution)/shard_map/all_gather | solution.py:101
  152.7 1.6 fusion
  154.4 0.5 convolution_bitcast_fusion
  155.2 0.5 convolution_convert_fusion.2
  155.7 41.6 %all_gather.18 = bf16[256,512]{0,1:T(8,128)(2,1)S(1)} all-gather(bf16[256,16]{0,1:T(8,128)(2,1)S(1)} %convolution_convert_fusion.2), channel_id=1, replica_groups=mesh['dp'=16,'tensor'=32] {'tensor'}, dimensions={1}, use_global_device_ids=true | all-gather | bytes 270336 | tf_op jit(solution)/shard_map/all_gather | solution.py:113
  197.3 0.5 convolution_convert_fusion.3
  197.8 38.9 %all_gather.17 = bf16[256,512]{0,1:T(8,128)(2,1)S(1)} all-gather(bf16[256,16]{0,1:T(8,128)(2,1)S(1)} %convolution_convert_fusion.3), channel_id=1, replica_groups=mesh['dp'=16,'tensor'=32] {'tensor'}, dimensions={1}, use_global_device_ids=true | all-gather | bytes 270336 | tf_op jit(solution)/shard_map/all_gather | solution.py:112
  236.9 0.3 fusion.82
  237.2 0.3 fusion.83
  237.6 0.2 select_reduce_fusion.1
  237.8 0.2 select_reduce_fusion
  239.0 0.2 fusion.10
  239.2 0.2 fusion.12
  239.6 1.5 convolution_convert_fusion.1
  241.2 147.0 %reduce-scatter.3.cloned.1.call-done = bf16[256,64]{0,1:T(8,128)(2,1)} async-done(((bf16[256,2048]{0,1:T(8,128)(2,1)}), bf16[256,64]{0,1:T(8,128)(2,1)}) %reduce-scatter.3.cloned.1.call-update) | async-done | bytes 32784 | tf_op jit(solution)/shard_map/reduce_scatter | solution.py:193
  388.2 1.4 add_convert_fusion
  389.7 59.4 %all-gather.5.cloned.1.call-done = bf16[256,2048]{0,1:T(8,128)(2,1)} async-done(((bf16[256,64]{0,1:T(8,128)(2,1)}), bf16[256,2048]{0,1:T(8,128)(2,1)}) %all-gather.5.cloned.1.call-update) | async-done | bytes 1048592 | tf_op jit(solution)/shard_map/all_gather | solution.py:197
  449.2 1.6 fusion.3
  450.8 2.1 fusion.15
  452.9 4.1 convolution_convert_fusion
  457.1 148.6 %reduce-scatter.5.cloned.1.call-done = bf16[256,64]{0,1:T(8,128)(2,1)} async-done(((bf16[256,2048]{0,1:T(8,128)(2,1)}), bf16[256,64]{0,1:T(8,128)(2,1)}) %reduce-scatter.5.cloned.1.call-update) | async-done | bytes 32784 | tf_op jit(solution)/shard_map/reduce_scatter | solution.py:203
  605.6 0.8 select_convert_fusion
  606.6 0.7 reshape.708
  607.3 10.2 %all-to-all-start.2 = ((bf16[16,2,512]{2,1,0:T(2,128)(2,1)}), bf16[16,2,512]{2,1,0:T(2,128)(2,1)S(1)}, u32[]{:S(2)}, u32[]{:S(2)}) async-start(bf16[16,2,512]{2,1,0:T(2,128)(2,1)} %reshape.708), calls=%async_computation.4 | async-start | bytes 65536 | tf_op jit(solution)/shard_map/all_to_all | solution.py:212
  617.5 0.6 copy.73
  618.1 0.6 copy.74
  618.7 9.9 %all-to-all-done.2 = bf16[16,2,512]{2,1,0:T(2,128)(2,1)S(1)} async-done(((bf16[16,2,512]{2,1,0:T(2,128)(2,1)}), bf16[16,2,512]{2,1,0:T(2,128)(2,1)S(1)}, u32[]{:S(2)}, u32[]{:S(2)}) %all-to-all-start.2) | async-done | bytes 32800 | tf_op jit(solution)/shard_map/all_to_all | solution.py:212
  628.8 1.5 scatter_fusion
  630.3 0.6 copy-done.7
  (103 shorter events, 3.3 us)
Async XLA Ops:
  7.2 445.7 %copy-start = (bf16[256,2048]{1,0:T(8,128)(2,1)S(1)}, bf16[256,2048]{1,0:T(8,128)(2,1)}, u32[]{:S(2)}) copy-start(bf16[256,2048]{1,0:T(8,128)(2,1)} %param.39) | copy-start | bytes 3145732
  7.2 4.1 copy-start.1
  7.2 4.7 copy-start.9
  8.6 20.9 %copy-start.10 = (bf16[1,8,1024]{2,1,0:T(8,128)(2,1)S(1)}, bf16[1,8,1024]{2,1,0:T(8,128)(2,1)}, u32[]{:S(2)}) copy-start(bf16[1,8,1024]{2,1,0:T(8,128)(2,1)} %param.30) | copy-start | bytes 49156
  9.9 68.6 %copy-start.13 = (s32[32]{0:T(128)S(1)}, s32[32]{0:T(128)}, u32[]{:S(2)}) copy-start(s32[32]{0:T(128)} %constant.238) | copy-start | bytes 388
  13.6 66.9 %all-to-all-start = ((bf16[16,2,512]{2,1,0:T(2,128)(2,1)}), bf16[16,2,512]{2,1,0:T(2,128)(2,1)S(1)}, u32[]{:S(2)}, u32[]{:S(2)}) async-start(bf16[16,2,512]{2,1,0:T(2,128)(2,1)} %reshape.706), calls=%async_computation | async-start | bytes 65536 | tf_op jit(solution)/shard_map/all_to_all | solution.py:15
  80.4 7.7 %copy-start.2 = (s32[16]{0:T(128)S(1)}, s32[16]{0:T(128)}, u32[]{:S(2)}) copy-start(s32[16]{0:T(128)} %param.28) | copy-start | bytes 196
  80.4 11.5 %copy-start.11 = (bf16[2048]{0:T(1024)(128)(2,1)S(1)}, bf16[2048]{0:T(1024)(128)(2,1)}, u32[]{:S(2)}) copy-start(bf16[2048]{0:T(1024)(128)(2,1)} %param.31) | copy-start | bytes 12292
  80.4 34.5 %all-to-all-start.1 = ((bf16[16,8,32,128]{3,1,0,2:T(8,128)(2,1)}), bf16[16,8,32,128]{3,1,0,2:T(8,128)(2,1)S(1)}, u32[]{:S(2)}, u32[]{:S(2)}) async-start(bf16[16,8,32,128]{3,1,0,2:T(8,128)(2,1)} %bitcast.23), calls=%async_computation.1 | async-start | bytes 2097152 | tf_op jit(solution)/shard_map/all_to_all | solution.py:159
  87.1 65.6 %all-gather.3.cloned.1.call-start = ((), (), s32[]{:S(2)}) async-start(), calls=%async_computation.5 | async-start | bytes 1081344 | tf_op jit(solution)/shard_map/all_gather | solution.py:101
  88.0 300.2 %reduce-scatter.3.cloned.1.call-start = ((), (), s32[]{:S(2)}) async-start(), calls=%async_computation.6 | async-start | bytes 1081344 | tf_op jit(solution)/shard_map/reduce_scatter | solution.py:193
  115.2 39.2 %copy-start.14 = (bf16[2048,64]{0,1:T(8,128)(2,1)S(1)}, bf16[2048,64]{0,1:T(8,128)(2,1)}, u32[]{:S(2)}) copy-start(bf16[2048,64]{0,1:T(8,128)(2,1)} %param.32) | copy-start | bytes 786436
  152.7 1.6 copy-start.3
  154.4 0.8 copy-start.15
  155.2 42.1 %copy-start.16 = (bf16[2048,16]{0,1:T(8,128)(2,1)S(1)}, bf16[2048,16]{0,1:T(8,128)(2,1)}, u32[]{:S(2)}) copy-start(bf16[2048,16]{0,1:T(8,128)(2,1)} %param.33) | copy-start | bytes 196612
  237.6 2.1 copy-start.8
  239.6 148.6 %copy-start.5 = (bf16[256,64]{0,1:T(8,128)(2,1)S(1)}, bf16[256,64]{0,1:T(8,128)(2,1)}, u32[]{:S(2)}) copy-start(bf16[256,64]{0,1:T(8,128)(2,1)} %copy.51) | copy-start | bytes 98308
  239.6 150.1 %copy-start.12 = (bf16[2048]{0:T(1024)(128)(2,1)S(1)}, bf16[2048]{0:T(1024)(128)(2,1)}, u32[]{:S(2)}) copy-start(bf16[2048]{0:T(1024)(128)(2,1)} %param.36) | copy-start | bytes 12292
  241.1 208.0 %all-gather.5.cloned.1.call-start = ((), (), s32[]{:S(2)}) async-start(), calls=%async_computation.7 | async-start | bytes 1081344 | tf_op jit(solution)/shard_map/all_gather | solution.py:197
  389.6 216.0 %reduce-scatter.5.cloned.1.call-start = ((), (), s32[]{:S(2)}) async-start(), calls=%async_computation.8 | async-start | bytes 1081344 | tf_op jit(solution)/shard_map/reduce_scatter | solution.py:203
  449.2 1.6 copy-start.4
  457.0 148.7 %copy-start.6 = (bf16[256,64]{0,1:T(8,128)(2,1)S(1)}, bf16[256,64]{0,1:T(8,128)(2,1)}, u32[]{:S(2)}) copy-start(bf16[256,64]{0,1:T(8,128)(2,1)} %add_convert_fusion) | copy-start | bytes 98308
  607.3 21.3 %all-to-all-start.2 = ((bf16[16,2,512]{2,1,0:T(2,128)(2,1)}), bf16[16,2,512]{2,1,0:T(2,128)(2,1)S(1)}, u32[]{:S(2)}, u32[]{:S(2)}) async-start(bf16[16,2,512]{2,1,0:T(2,128)(2,1)} %reshape.708), calls=%async_computation.4 | async-start | bytes 65536 | tf_op jit(solution)/shard_map/all_to_all | solution.py:212
  630.3 0.6 copy-start.7
Sparse Core Ops, SparseCore 0:
  90.6 62.0 all-gather.2
  241.3 146.9 reduce-scatter.2
  391.0 58.1 all-gather.4
  457.1 148.4 reduce-scatter.4
